TPU v7x, 512 devices: a whole 4x4x16 slice. The times are simulated.
512 devices in a mesh: ctx: 64 (over y, z), kvh: 8 (over x, core).
Axes of the slice: x: 4, y: 4, z: 16, core: 2. Of those that a mesh axis runs over, the one named last changes fastest.
Arguments:
- queries: bfloat16 [16384, 8192], P('ctx', 'kvh'), may hold values from -256 to 256
- keys: bfloat16 [16384, 1024], P('ctx', 'kvh'), may hold values from -4 to 4
- values: bfloat16 [16384, 1024], P('ctx', 'kvh'), may hold values from -6 to 6
- selection: int32 [8, 256, 16], P('kvh', 'ctx'), may hold values from -1 to 250, as said below
Outputs:
- attention_out: bfloat16 [16384, 8192], P(('ctx', 'kvh'))
Inputs may be any that keep to these rules, and one draw needn't show every extreme that they name: `selection`: entries -1 stand after the named tiles; the tiles of one list are distinct and each is at most b - 256 / 64 - 1 for block b. The query blocks held by one index of ctx (blocks c * 4 to (c + 1) * 4 - 1) name, together, at most 2 distinct tiles of any one other such group of blocks, and only tiles of earlier groups; some group reaches 2 in every draw.
All inputs are finite; a program needn't handle non-finite values.
Results may differ from a plain program's by a relative error of at most 0.008.
Values may be sent and summed in bfloat16 or wider, within the bound.
No kernel may reach another device: no remote copies, remote signals or barrier semaphores. Data moves between devices by JAX's collectives and lax.ppermute only.
A program may use at most 64 MiB of HBM per device.

v0:
```python
import jax
import jax.numpy as jnp
from jax import lax
from jax.sharding import PartitionSpec as P

TILE = 64
SEL = 16
WINDOW = 256
masked_score = -1e30


def passed_along(value, axis, steps):
    count = lax.axis_size(axis)
    first, last = (max(0, -steps), min(count, count - steps))
    return lax.ppermute(value, axis, [(source, source + steps) for source in range(first, last)])


def block_attention_step(
    query_rows, window_keys, window_values, window_ok, chosen_keys, chosen_values, chosen_ok, scale
):
    win_scores = (
        jnp.einsum("rhd,jd->hrj", query_rows, window_keys, preferred_element_type=jnp.float32)
        * scale
    )
    sel_scores = (
        jnp.einsum("rhd,jd->hrj", query_rows, chosen_keys, preferred_element_type=jnp.float32)
        * scale
    )
    win_scores = jnp.where(window_ok[None, :, :], win_scores, masked_score)
    sel_scores = jnp.where(chosen_ok[None, None, :], sel_scores, masked_score)
    peak = jnp.maximum(jnp.max(win_scores, axis=-1), jnp.max(sel_scores, axis=-1))
    win_weights = jnp.exp(win_scores - peak[:, :, None])
    sel_weights = jnp.exp(sel_scores - peak[:, :, None])
    total = jnp.sum(win_weights, axis=-1) + jnp.sum(sel_weights, axis=-1)
    numerator = jnp.einsum(
        "hrj,jd->rhd",
        win_weights.astype(jnp.bfloat16),
        window_values,
        preferred_element_type=jnp.float32,
    )
    numerator = numerator + jnp.einsum(
        "hrj,jd->rhd",
        sel_weights.astype(jnp.bfloat16),
        chosen_values,
        preferred_element_type=jnp.float32,
    )
    result = numerator / jnp.transpose(total)[:, :, None]
    return result.astype(jnp.bfloat16).reshape(query_rows.shape[0], -1)


def per_device(queries, keys, values, selection):
    tok_rows = queries.shape[0]
    head_size = keys.shape[1]
    per_dev = tok_rows // TILE
    here = lax.axis_index("ctx")
    scale = 1.0 / head_size**0.5
    tile_width = TILE * head_size
    flat_list = selection[0].reshape(-1)
    listed = flat_list >= 0
    safe_list = jnp.maximum(flat_list, 0)
    earlier_keys, earlier_values = passed_along((keys, values), "ctx", 1)
    window_keys = jnp.concatenate([earlier_keys, keys], axis=0)
    window_values = jnp.concatenate([earlier_values, values], axis=0)
    piece_keys = lax.all_gather(keys, "ctx", axis=0, tiled=True)
    piece_values = lax.all_gather(values, "ctx", axis=0, tiled=True)
    count = piece_keys.shape[0] // TILE
    piece_tiles = jnp.concatenate(
        [piece_keys.reshape(count, tile_width), piece_values.reshape(count, tile_width)], axis=1
    )
    picker = (safe_list[:, None] == jnp.arange(count, dtype=jnp.int32)[None, :]).astype(
        jnp.bfloat16
    )
    chosen = jnp.dot(picker, piece_tiles, preferred_element_type=jnp.float32).astype(jnp.bfloat16)
    chosen_keys = chosen[:, :tile_width].reshape(per_dev, SEL * TILE, head_size)
    chosen_values = chosen[:, tile_width:].reshape(per_dev, SEL * TILE, head_size)
    chosen_ok = jnp.repeat(listed.reshape(per_dev, SEL), TILE, axis=1)
    key_pos = here * tok_rows - tok_rows + jnp.arange(2 * tok_rows, dtype=jnp.int32)
    block_queries = queries.reshape(per_dev, TILE, -1, head_size)

    def one_block(inner):
        block_index, block_rows, block_keys, block_values, block_ok = inner
        query_pos = here * tok_rows + block_index * TILE + jnp.arange(TILE, dtype=jnp.int32)
        window_ok = (
            (key_pos[None, :] <= query_pos[:, None])
            & (key_pos[None, :] > query_pos[:, None] - WINDOW)
            & (key_pos[None, :] >= 0)
        )
        return block_attention_step(
            block_rows,
            window_keys,
            window_values,
            window_ok,
            block_keys,
            block_values,
            block_ok,
            scale,
        )

    attended = lax.map(
        one_block,
        (
            jnp.arange(per_dev, dtype=jnp.int32),
            block_queries,
            chosen_keys,
            chosen_values,
            chosen_ok,
        ),
    )
    attended = attended.reshape(tok_rows, -1)
    return lax.all_to_all(attended, "kvh", split_axis=0, concat_axis=1, tiled=True)


def solution(mesh):
    return jax.shard_map(
        per_device,
        mesh=mesh,
        in_specs=(P("ctx", "kvh"), P("ctx", "kvh"), P("ctx", "kvh"), P("kvh", "ctx", None)),
        out_specs=P(("ctx", "kvh"), None),
        check_vma=False,
    )
```

profile of v0, /device:TPU:1, one launch (start us, length us, event | category | flops | bytes accessed | tf_op | source)
XLA Modules:
  0.0 379.2 jit_solution(10833743811720009542)
XLA Ops:
  6.5 0.7 all-gather.3.cloned.1.call-update
  7.3 0.7 all-gather.5.cloned.1.call-update
  8.0 4.4 %collective-permute-start = (bf16[256,128]{1,0:T(8,128)(2,1)}, bf16[256,128]{1,0:T(8,128)(2,1)S(1)}, u32[]{:S(2)}, u32[]{:S(2)}) collective-permute-start(bf16[256,128]{1,0:T(8,128)(2,1)} %param.7), channel_id=1, source_target_pairs={{0,8},{8,16},{16,24},{24,32},{32,40},{40,48},{48,56},{56,64},{64,7... | collective-permute-start | bytes 196616 | tf_op jit(solution)/shard_map/ppermute | solution.py:15
  12.4 3.5 collective-permute-start.1
  15.9 0.7 broadcast_maximum_fusion
  16.6 0.7 compare_bitcast_fusion
  17.4 2.0 copy.42
  19.5 0.1 reshape.135
  19.6 0.9 pad_maximum_fusion
  20.4 0.9 pad_maximum_fusion.1
  21.3 132.8 %all-gather.3.cloned.1.call-done = bf16[16384,128]{1,0:T(8,128)(2,1)} async-done(((bf16[256,128]{1,0:T(8,128)(2,1)}), bf16[16384,128]{1,0:T(8,128)(2,1)}) %all-gather.3.cloned.1.call-update) | async-done | bytes 4194320 | tf_op jit(solution)/shard_map/all_gather | solution.py:64
  154.1 7.3 %reshape.136 = bf16[256,8192]{1,0:T(8,128)(2,1)} reshape(bf16[16384,128]{1,0:T(8,128)(2,1)} %all-gather.3.cloned.1.call-done) | data formatting | bytes 8388608 | tf_op jit(solution)/shard_map/reshape | solution.py:68
  161.5 136.8 %all-gather.5.cloned.1.call-done = bf16[16384,128]{1,0:T(8,128)(2,1)} async-done(((bf16[256,128]{1,0:T(8,128)(2,1)}), bf16[16384,128]{1,0:T(8,128)(2,1)}) %all-gather.5.cloned.1.call-update) | async-done | bytes 4194320 | tf_op jit(solution)/shard_map/all_gather | solution.py:65
  298.3 7.3 %reshape.137 = bf16[256,8192]{1,0:T(8,128)(2,1)} reshape(bf16[16384,128]{1,0:T(8,128)(2,1)} %all-gather.5.cloned.1.call-done) | data formatting | bytes 8388608 | tf_op jit(solution)/shard_map/reshape | solution.py:68
  305.6 5.1 %convolution_convert_fusion = bf16[64,16384]{1,0:T(8,128)(2,1)S(1)} fusion(bf16[256,8192]{1,0:T(8,128)(2,1)} %reshape.137, bf16[256,8192]{1,0:T(8,128)(2,1)} %reshape.136, s32[64]{0:T(128)S(1)} %max.21), kind=kOutput, calls=%fused_computation.43 | convolution fusion | flops 554713088 | bytes 10486016 | tf_op jit(solution)/shard_map/dot_general | solution.py:73
  310.7 0.2 fusion.35
  310.9 1.3 reshape.138
  312.2 1.3 reshape.139
  313.5 35.6 %while.13 = (s32[]{:T(128)}, bf16[4,64,1024]{2,1,0:T(8,128)(2,1)}, s32[4]{0:T(128)S(1)}, s32[]{:T(128)}, bf16[4,64,8,128]{3,2,1,0:T(8,128)(2,1)}, /*index=5*/bf1...) while((s32[]{:T(128)}, bf16[4,64,1024]{2,1,0:T(8,128)(2,1)}, ...), condition=%wide.region_5.6_spmd.clone, body=%wide.region_0.5_spmd.clone.sunk | while | flops 410321536 | bytes 14410449 | solution.py:99
  313.5 0.6 dynamic_slice.60
  314.8 0.1 and_and_fusion.2
  314.9 0.9 dynamic-slice_bitcast_fusion.2
  315.8 0.4 fusion.51
  316.3 1.5 bitcast_reduce_fusion.2
  317.8 0.5 fusion.53
  318.6 1.0 fusion.52
  319.6 1.6 convolution_bitcast_fusion.3
  321.2 0.3 fusion.54
  321.6 0.1 copy.62
  321.7 0.7 constant_dynamic-update-slice_fusion.2
  322.4 0.6 dynamic_slice.60
  323.7 0.1 and_and_fusion.2
  323.8 0.9 dynamic-slice_bitcast_fusion.2
  324.7 0.4 fusion.51
  325.2 1.5 bitcast_reduce_fusion.2
  326.7 0.5 fusion.53
  327.5 1.0 fusion.52
  328.6 1.6 convolution_bitcast_fusion.3
  330.1 0.3 fusion.54
  330.5 0.1 copy.62
  330.6 0.7 constant_dynamic-update-slice_fusion.2
  331.3 0.6 dynamic_slice.60
  332.6 0.1 and_and_fusion.2
  332.7 0.9 dynamic-slice_bitcast_fusion.2
  333.6 0.4 fusion.51
  334.2 1.5 bitcast_reduce_fusion.2
  335.6 0.5 fusion.53
  336.4 1.0 fusion.52
  337.5 1.6 convolution_bitcast_fusion.3
  339.1 0.3 fusion.54
  339.6 0.7 constant_dynamic-update-slice_fusion.2
  340.2 0.6 dynamic_slice.60
  341.5 0.1 and_and_fusion.2
  341.6 0.9 dynamic-slice_bitcast_fusion.2
  342.5 0.4 fusion.51
  343.1 1.5 bitcast_reduce_fusion.2
  344.6 0.5 fusion.53
  345.3 1.0 fusion.52
  346.4 1.6 convolution_bitcast_fusion.3
  348.0 0.3 fusion.54
  348.3 0.1 copy.62
  348.5 0.7 constant_dynamic-update-slice_fusion.2
  349.1 22.4 %all_to_all.19 = bf16[8,32,1024]{2,1,0:T(8,128)(2,1)S(1)} all-to-all(bf16[8,32,1024]{2,1,0:T(8,128)(2,1)} %bitcast.83), channel_id=1, replica_groups=mesh['ctx'=64,'kvh'=8] {'kvh'}, dimensions={0} | all-to-all | bytes 1048576 | tf_op jit(solution)/shard_map/all_to_all | solution.py:110
  371.5 0.8 copy.41
  (61 shorter events, 2.0 us)
Async XLA Ops:
  6.5 147.6 %all-gather.3.cloned.1.call-start = ((), (), s32[]{:S(2)}) async-start(), calls=%async_computation.1 | async-start | bytes 4259840 | tf_op jit(solution)/shard_map/all_gather | solution.py:64
  7.3 291.0 %all-gather.5.cloned.1.call-start = ((), (), s32[]{:S(2)}) async-start(), calls=%async_computation.2 | async-start | bytes 4259840 | tf_op jit(solution)/shard_map/all_gather | solution.py:65
  8.0 11.5 %collective-permute-start = (bf16[256,128]{1,0:T(8,128)(2,1)}, bf16[256,128]{1,0:T(8,128)(2,1)S(1)}, u32[]{:S(2)}, u32[]{:S(2)}) collective-permute-start(bf16[256,128]{1,0:T(8,128)(2,1)} %param.7), channel_id=1, source_target_pairs={{0,8},{8,16},{16,24},{24,32},{32,40},{40,48},{48,56},{56,64},{64,7... | collective-permute-start | bytes 196616 | tf_op jit(solution)/shard_map/ppermute | solution.py:15
  12.4 8.0 %collective-permute-start.1 = (bf16[256,128]{1,0:T(8,128)(2,1)}, bf16[256,128]{1,0:T(8,128)(2,1)S(1)}, u32[]{:S(2)}, u32[]{:S(2)}) collective-permute-start(bf16[256,128]{1,0:T(8,128)(2,1)} %param.8), channel_id=1, source_target_pairs={{0,8},{8,16},{16,24},{24,32},{32,40},{40,48},{48,56},{56,64},{64,7... | collective-permute-start | bytes 196616 | tf_op jit(solution)/shard_map/ppermute | solution.py:15
  319.6 1.7 copy-start
  328.5 1.7 copy-start
  337.4 1.7 copy-start
  346.3 1.7 copy-start
Sparse Core Ops, SparseCore 0:
  10.3 143.7 all-gather.2
  157.1 141.1 all-gather.4
where the time goes:
time: 380 us; the launch traced here: 379 us
  waiting for transfers between devices  271 us (71%)
  local copies, waits for them, and re-layouts  31.2 us (8%)
  blocking collectives  22.4 us (6%)
  matrix products  20.4 us (5%)
  between operations  13.5 us (4%)
  other arithmetic  9.84 us (3%)
  starting transfers between devices  7.96 us (2%)
    all_gather x1, waiting for transfers between devices, per_device(): piece_values = lax.all_gather(values, 'ctx', axis=0, tiled=True)  137 us
    all_gather x1, waiting for transfers between devices, per_device(): piece_keys = lax.all_gather(keys, 'ctx', axis=0, tiled=True)  133 us
    all_to_all x1, blocking collectives, per_device(): lax.all_to_all(attended, 'kvh', split_axis=0, concat_axis=1, tiled=True)  22.4 us
    ppermute x2, starting transfers between devices, passed_along(): lax.ppermute(value, axis, [(source, source + steps) for source in range(f...  7.92 us
  transfers between devices with their start and end apart: 4, of which 2 were waited for; matrix products, arithmetic and copies ran while one was open for 3% of the time, Pallas kernels for 0%

commit v1 on v0

--- a/solution.py
+++ b/solution.py
@@ -61,7 +61,15 @@
     earlier_keys, earlier_values = passed_along((keys, values), "ctx", 1)
     window_keys = jnp.concatenate([earlier_keys, keys], axis=0)
     window_values = jnp.concatenate([earlier_values, values], axis=0)
-    piece_keys = lax.all_gather(keys, "ctx", axis=0, tiled=True)
+    piece_keys = jnp.concatenate(
+        lax.all_to_all(
+            jnp.stack(tuple((keys for _ in range(lax.axis_size("ctx")))), 0),
+            axis_name="ctx",
+            split_axis=0,
+            concat_axis=0,
+        ),
+        0,
+    )
     piece_values = lax.all_gather(values, "ctx", axis=0, tiled=True)
     count = piece_keys.shape[0] // TILE
     piece_tiles = jnp.concatenate(

time: 380 us -> 333 us (0.88)
  waiting for transfers between devices: 271 us -> 212 us
  starting transfers between devices: 7.96 us -> 25.7 us
  blocking collectives: 22.4 us -> 16.5 us
    ppermute x2, waiting for transfers between devices: 0.01 us -> 192 us  [passed_along(): lax.ppermute(value, axis, [(source, source + steps) for source in range(f...]
    all_gather x1 -> x0, waiting for transfers between devices: 133 us -> none  [per_device(): piece_keys = lax.all_gather(keys, 'ctx', axis=0, tiled=True)]
    all_gather x1, waiting for transfers between devices: 137 us -> 20.1 us  [per_device(): piece_values = lax.all_gather(values, 'ctx', axis=0, tiled=True)]
    all_to_all x0 -> x1, starting transfers between devices: none -> 19.7 us  [per_device(): lax.all_to_all(jnp.stack(tuple((keys for _ in range(lax.axis_size('ctx'))...]
    another operation x0 -> x2, local copies, waits for them, and re-layouts: none -> 11.2 us  [the longest x1 7.34 us: per_device(): piece_keys.reshape(count, tile_width)]
    reshape x1 -> x0, local copies, waits for them, and re-layouts: 7.33 us -> none  [per_device(): piece_keys.reshape(count, tile_width)]
    all_to_all x1, blocking collectives: 22.4 us -> 16.5 us  [per_device(): lax.all_to_all(attended, 'kvh', split_axis=0, concat_axis=1, tiled=True)]
  transfers between devices with their start and end apart: 4 -> 4, of which waited for: 2 -> 3; matrix products, arithmetic and copies ran while one was open for 3% -> 3% of each run, Pallas kernels for 0% -> 0%
where the time goes in v1:
time: 333 us; the launch traced here: 332 us
  waiting for transfers between devices  212 us (64%)
  local copies, waits for them, and re-layouts  34 us (10%)
  starting transfers between devices  25.7 us (8%)
  matrix products  20.4 us (6%)
  blocking collectives  16.5 us (5%)
  between operations  13.5 us (4%)
  other arithmetic  6.8 us (2%)
    ppermute x2, waiting for transfers between devices, passed_along(): lax.ppermute(value, axis, [(source, source + steps) for source in range(f...  192 us
    all_gather x1, waiting for transfers between devices, per_device(): piece_values = lax.all_gather(values, 'ctx', axis=0, tiled=True)  20.1 us
    all_to_all x1, starting transfers between devices, per_device(): lax.all_to_all(jnp.stack(tuple((keys for _ in range(lax.axis_size('ctx'))...  19.7 us
    all_to_all x1, blocking collectives, per_device(): lax.all_to_all(attended, 'kvh', split_axis=0, concat_axis=1, tiled=True)  16.5 us
    another operation x1, local copies, waits for them, and re-layouts, per_device(): piece_keys.reshape(count, tile_width)  7.34 us
    reshape x1, local copies, waits for them, and re-layouts, per_device(): piece_values.reshape(count, tile_width)  7.31 us
  transfers between devices with their start and end apart: 4, of which 3 were waited for; matrix products, arithmetic and copies ran while one was open for 3% of the time, Pallas kernels for 0%

profile of v1, /device:TPU:1, one launch (start us, length us, event | category | flops | bytes accessed | tf_op | source)
XLA Modules:
  0.0 332.2 jit_solution(14544985331312795942)
XLA Ops:
  6.5 3.8 %stack.2 = bf16[64,256,128]{2,1,0:T(8,128)(2,1)} broadcast(bf16[256,128]{1,0:T(8,128)(2,1)} %param.7), dimensions={1,2} | broadcast | bytes 4259840 | tf_op jit(solution)/shard_map/stack | solution.py:66
  10.4 19.7 %all-to-all-start = ((bf16[64,256,128]{2,1,0:T(8,128)(2,1)}), bf16[64,256,128]{2,1,0:T(8,128)(2,1)}, u32[]{:S(2)}, u32[]{:S(2)}) async-start(bf16[64,256,128]{2,1,0:T(8,128)(2,1)} %stack.2), calls=%async_computation | async-start | bytes 8388608 | tf_op jit(solution)/shard_map/all_to_all | solution.py:65
  30.1 0.7 all-gather.2.cloned.1.call-update
  30.8 2.8 collective-permute-start
  33.7 3.1 collective-permute-start.1
  36.9 0.9 copy.42
  37.9 0.1 reshape.134
  38.0 186.6 %collective-permute-done = bf16[256,128]{1,0:T(8,128)(2,1)S(1)} collective-permute-done((bf16[256,128]{1,0:T(8,128)(2,1)S(1)}, bf16[256,128]{1,0:T(8,128)(2,1)S(1)}, u32[]{:S(2)}, u32[]{:S(2)}) %collective-permute-start) | collective-permute-done | bytes 65568 | tf_op jit(solution)/shard_map/ppermute | solution.py:15
  224.6 5.1 %collective-permute-done.1 = bf16[256,128]{1,0:T(8,128)(2,1)S(1)} collective-permute-done((bf16[256,128]{1,0:T(8,128)(2,1)S(1)}, bf16[256,128]{1,0:T(8,128)(2,1)S(1)}, u32[]{:S(2)}, u32[]{:S(2)}) %collective-permute-start.1) | collective-permute-done | bytes 65568 | tf_op jit(solution)/shard_map/ppermute | solution.py:15
  229.6 20.1 %all-gather.2.cloned.1.call-done = bf16[16384,128]{1,0:T(8,128)(2,1)} async-done(((bf16[256,128]{1,0:T(8,128)(2,1)}), bf16[16384,128]{1,0:T(8,128)(2,1)}) %all-gather.2.cloned.1.call-update) | async-done | bytes 4194320 | tf_op jit(solution)/shard_map/all_gather | solution.py:73
  249.7 7.3 %reshape.135 = bf16[256,8192]{1,0:T(8,128)(2,1)} reshape(bf16[16384,128]{1,0:T(8,128)(2,1)} %all-gather.2.cloned.1.call-done) | data formatting | bytes 8388608 | tf_op jit(solution)/shard_map/reshape | solution.py:76
  257.1 7.3 %reshape_reshape.3 = bf16[256,8192]{1,0:T(8,128)(2,1)} reshape(bf16[64,256,128]{2,1,0:T(8,128)(2,1)} %all-to-all-done) | data formatting | bytes 8388608 | tf_op jit(solution)/shard_map/reshape;reshape | solution.py:76
  264.4 5.1 %convolution_convert_fusion = bf16[64,16384]{1,0:T(8,128)(2,1)S(1)} fusion(bf16[256,8192]{1,0:T(8,128)(2,1)} %reshape.135, bf16[256,8192]{1,0:T(8,128)(2,1)} %reshape_reshape.3, s32[64]{0:T(128)S(1)} %max.21), kind=kOutput, calls=%fused_computation.43 | convolution fusion | flops 554713088 | bytes 10486016 | tf_op jit(solution)/shard_map/dot_general | solution.py:81
  269.5 0.2 fusion.35
  269.7 1.3 reshape.136
  271.0 1.3 reshape.137
  272.2 35.8 %while.13 = (s32[]{:T(128)}, bf16[4,64,1024]{2,1,0:T(8,128)(2,1)}, s32[4]{0:T(128)S(1)}, s32[]{:T(128)}, bf16[4,64,8,128]{3,2,1,0:T(8,128)(2,1)}, /*index=5*/bf1...) while((s32[]{:T(128)}, bf16[4,64,1024]{2,1,0:T(8,128)(2,1)}, ...), condition=%wide.region_5.6_spmd.clone, body=%wide.region_0.5_spmd.clone.sunk | while | flops 410321536 | bytes 14410449 | solution.py:107
  272.2 0.6 dynamic_slice.60
  273.6 0.1 and_and_fusion.2
  273.7 0.9 dynamic-slice_bitcast_fusion.2
  274.6 0.4 fusion.51
  275.1 1.5 bitcast_reduce_fusion.2
  276.6 0.5 fusion.53
  277.2 0.1 copy.60
  277.3 1.0 fusion.52
  278.4 1.6 convolution_bitcast_fusion.3
  280.0 0.3 fusion.54
  280.4 0.1 copy.62
  280.5 0.7 constant_dynamic-update-slice_fusion.2
  281.2 0.6 dynamic_slice.60
  282.5 0.1 and_and_fusion.2
  282.6 0.9 dynamic-slice_bitcast_fusion.2
  283.5 0.4 fusion.51
  284.1 1.5 bitcast_reduce_fusion.2
  285.6 0.5 fusion.53
  286.3 1.0 fusion.52
  287.4 1.6 convolution_bitcast_fusion.3
  289.0 0.3 fusion.54
  289.3 0.1 copy.62
  289.5 0.7 constant_dynamic-update-slice_fusion.2
  290.1 0.6 dynamic_slice.60
  291.4 0.1 and_and_fusion.2
  291.5 0.9 dynamic-slice_bitcast_fusion.2
  292.5 0.4 fusion.51
  293.0 1.5 bitcast_reduce_fusion.2
  294.5 0.5 fusion.53
  295.2 1.0 fusion.52
  296.3 1.6 convolution_bitcast_fusion.3
  297.9 0.3 fusion.54
  298.2 0.1 copy.62
  298.4 0.7 constant_dynamic-update-slice_fusion.2
  299.1 0.6 dynamic_slice.60
  300.4 0.1 and_and_fusion.2
  300.5 0.9 dynamic-slice_bitcast_fusion.2
  301.4 0.4 fusion.51
  301.9 1.5 bitcast_reduce_fusion.2
  303.4 0.5 fusion.53
  304.2 1.0 fusion.52
  305.3 1.6 convolution_bitcast_fusion.3
  306.9 0.3 fusion.54
  307.2 0.1 copy.62
  307.4 0.7 constant_dynamic-update-slice_fusion.2
  308.0 16.5 %all_to_all.24 = bf16[8,32,1024]{2,1,0:T(8,128)(2,1)S(1)} all-to-all(bf16[8,32,1024]{2,1,0:T(8,128)(2,1)} %bitcast.83), channel_id=1, replica_groups=mesh['ctx'=64,'kvh'=8] {'kvh'}, dimensions={0} | all-to-all | bytes 1048576 | tf_op jit(solution)/shard_map/all_to_all | solution.py:118
  324.5 0.8 copy.41
  (69 shorter events, 1.8 us)
Async XLA Ops:
  10.4 20.4 %copy-start.2 = (bf16[256,128]{1,0:T(8,128)(2,1)S(1)}, bf16[256,128]{1,0:T(8,128)(2,1)}, u32[]{:S(2)}) copy-start(bf16[256,128]{1,0:T(8,128)(2,1)} %param.7) | copy-start | bytes 196612
  10.4 23.3 %copy-start.3 = (bf16[256,128]{1,0:T(8,128)(2,1)S(1)}, bf16[256,128]{1,0:T(8,128)(2,1)}, u32[]{:S(2)}) copy-start(bf16[256,128]{1,0:T(8,128)(2,1)} %param.8) | copy-start | bytes 196612
  10.4 26.4 %copy-start.4 = (s32[1,4,16]{2,1,0:T(4,128)S(1)}, s32[1,4,16]{2,1,0:T(4,128)}, u32[]{:S(2)}) copy-start(s32[1,4,16]{2,1,0:T(4,128)} %param.9) | copy-start | bytes 772
  10.4 26.5 %copy-start.1 = (bf16[256,1024]{1,0:T(8,128)(2,1)S(1)}, bf16[256,1024]{1,0:T(8,128)(2,1)}, u32[]{:S(2)}) copy-start(bf16[256,1024]{1,0:T(8,128)(2,1)} %param.6) | copy-start | bytes 1572868
  10.4 246.7 %all-to-all-start = ((bf16[64,256,128]{2,1,0:T(8,128)(2,1)}), bf16[64,256,128]{2,1,0:T(8,128)(2,1)}, u32[]{:S(2)}, u32[]{:S(2)}) async-start(bf16[64,256,128]{2,1,0:T(8,128)(2,1)} %stack.2), calls=%async_computation | async-start | bytes 8388608 | tf_op jit(solution)/shard_map/all_to_all | solution.py:65
  30.1 219.7 %all-gather.2.cloned.1.call-start = ((), (), s32[]{:S(2)}) async-start(), calls=%async_computation.2 | async-start | bytes 4259840 | tf_op jit(solution)/shard_map/all_gather | solution.py:73
  30.8 193.7 %collective-permute-start = (bf16[256,128]{1,0:T(8,128)(2,1)S(1)}, bf16[256,128]{1,0:T(8,128)(2,1)S(1)}, u32[]{:S(2)}, u32[]{:S(2)}) collective-permute-start(bf16[256,128]{1,0:T(8,128)(2,1)S(1)} %copy-done.2), channel_id=1, source_target_pairs={{0,8},{8,16},{16,24},{24,32},{32,40},{40,48},{48,56},{56,64},{64,7... | collective-permute-start | bytes 196616 | tf_op jit(solution)/shard_map/ppermute | solution.py:15
  33.7 195.9 %collective-permute-start.1 = (bf16[256,128]{1,0:T(8,128)(2,1)S(1)}, bf16[256,128]{1,0:T(8,128)(2,1)S(1)}, u32[]{:S(2)}, u32[]{:S(2)}) collective-permute-start(bf16[256,128]{1,0:T(8,128)(2,1)S(1)} %copy-done.3), channel_id=1, source_target_pairs={{0,8},{8,16},{16,24},{24,32},{32,40},{40,48},{48,56},{56,64},{64,7... | collective-permute-start | bytes 196616 | tf_op jit(solution)/shard_map/ppermute | solution.py:15
  278.4 1.7 copy-start
  287.3 1.7 copy-start
  296.2 1.7 copy-start
  305.2 1.7 copy-start
Sparse Core Ops, SparseCore 0:
  33.8 215.8 all-gather.1
